TPU v7x, 32 devices: a whole 2x2x4 slice. The times are simulated.
32 devices in a mesh: groups: 2 (over y), space: 16 (over z, x, core).
Axes of the slice: x: 2, y: 2, z: 4, core: 2. Of those that a mesh axis runs over, the one named last changes fastest.
Arguments:
- field: float32 [64, 40, 8, 256], P(('groups', 'space')), parts along dimension 0, may hold values from -6 to 6
- grad_out: float32 [64, 40, 8, 256], P(('groups', 'space')), parts along dimension 0, may hold values from -6 to 6
- weight: float32 [256, 27, 256], P('space'), may hold values from -0.078125 to 0.078125
- bias: float32 [256], replicated, may hold values from -3 to 3
- land_bias: float32 [256], replicated, may hold values from -3 to 3
- level_gain: float32 [4, 256], replicated, may hold values from 0.5 to 1.5
- land_mask: int32 [32, 40], P('space'), may hold values 0 or 1
- level_index: int32 [8], replicated, may hold values from 0 to 3, as said below
Outputs:
- grad_field: float32 [64, 40, 8, 256], P(('groups', 'space')), parts along dimension 0
- grad_weight: float32 [512, 27, 256], P(('groups', 'space')), parts along dimension 0
- grad_bias: float32 [512], P('groups'), parts along dimension 0
- grad_land: float32 [512], P('groups'), parts along dimension 0
- grad_gain: float32 [8, 256], P('groups'), parts along dimension 0
There are 2 independent parts, one for each index of `groups`. A program takes and returns all parts, laid end to end along the dimension named above; an argument that names none is the same for every part. Nothing has to cross between parts.
Inputs may be any that keep to these rules, and one draw needn't show every extreme that they name: `level_index`: a gain table row for each level; every row of the table is used by some level.
All inputs are finite; a program needn't handle non-finite values. No bound on the sum of `land_mask` on one device may be relied on, other than what follows from the above.
Results may differ from a plain program's by a relative error of at most 0.00011.
Values sent between devices are 32-bit elements; how exact they have to be, the bound alone decides.
No kernel may reach another device: no remote copies, remote signals or barrier semaphores. Data moves between devices by JAX's collectives and lax.ppermute only.
A program may use at most 128 MiB of HBM per device.

v0:
```python
import jax
import jax.numpy as jnp
from jax import lax
from jax.sharding import PartitionSpec as P

highest = lax.Precision.HIGHEST
high = lax.Precision.HIGH


def with_halo(array, sides, width):
    for axis, dim in sides:
        count, length = (lax.axis_size(axis), array.shape[dim])
        up = [(i, (i + 1) % count) for i in range(count - 1)]
        down = [(j, i) for i, j in up]
        last = lax.slice_in_dim(array, length - width, length, axis=dim)
        leading = lax.slice_in_dim(array, 0, width, axis=dim)
        before = lax.ppermute(last, axis, up)
        after = lax.ppermute(leading, axis, down)
        array = jnp.concatenate([before, array, after], axis=dim)
    return array


def wrap_levels(field):
    wrapped = jnp.concatenate([field[:, -1:], field, field[:, :1]], axis=1)
    return jnp.pad(wrapped, ((0, 0), (0, 0), (1, 1), (0, 0)))


def window_table(grid, out_rows, flipped):
    lon_n = grid.shape[1] - 2
    lev_n = grid.shape[2] - 2
    chans = grid.shape[3]
    windows = []
    for offset in range(27):
        lat_off, remainder = divmod(offset, 9)
        lon_off, lev_off = divmod(remainder, 3)
        if flipped:
            lat_off, lon_off, lev_off = (2 - lat_off, 2 - lon_off, 2 - lev_off)
        window = grid[
            lat_off : lat_off + out_rows, lon_off : lon_off + lon_n, lev_off : lev_off + lev_n
        ]
        windows.append(window.reshape(-1, chans))
    return jnp.stack(windows, axis=1)


def conv_piece(table, piece):
    return jnp.einsum("rop,poc->rc", table, piece, precision=high)


def back_piece(table, piece):
    return jnp.einsum("roc,qoc->rq", table, piece, precision=high)


def stacked_product(delta_flat, table):
    d_hi, d_lo = split_bf16(delta_flat)
    t_hi, t_lo = split_bf16(table)
    lhs = jnp.concatenate([d_hi, d_hi, d_lo], axis=0)
    rhs = jnp.concatenate([t_hi, t_lo, t_hi], axis=0)
    return jnp.einsum("rq,rop->opq", lhs, rhs, preferred_element_type=jnp.float32)


def all_sum(x):
    count = lax.axis_size("space")
    if count & count - 1:
        return lax.psum(x, "space")
    bit = 1
    while bit < count:
        x = x + lax.ppermute(x, "space", [(i, i ^ bit) for i in range(count)])
        bit *= 2
    return x


def split_bf16(x):
    hi = lax.reduce_precision(x, exponent_bits=8, mantissa_bits=7)
    return (hi.astype(jnp.bfloat16), (x - hi).astype(jnp.bfloat16))


def per_device(field, grad_out, weight, bias, land_bias, level_gain, land_mask, level_index):
    rows, lon_n, lev_n, chans = field.shape
    land_float = land_mask.astype(jnp.float32)
    one_hot = (
        level_index[:, None] == jnp.arange(level_gain.shape[0], dtype=jnp.int32)[None, :]
    ).astype(jnp.float32)
    gains = jnp.dot(one_hot, level_gain, precision=highest)
    full_weight = lax.all_gather(weight, "space", axis=0, tiled=True)
    grid_pre = wrap_levels(with_halo(field, (("space", 0),), 1))
    table_pre = window_table(grid_pre, rows, False)
    conv = conv_piece(table_pre, full_weight)
    conv = conv.reshape(rows, lon_n, lev_n, chans)
    pre = conv + bias + land_float[:, :, None, None] * land_bias
    sigma = jax.nn.sigmoid(pre)
    active = pre * sigma
    delta = grad_out * gains * sigma * (1.0 + pre * (1.0 - sigma))
    delta_pad = with_halo(delta, (("space", 0),), 1)
    delta_table = window_table(wrap_levels(delta_pad), rows, True)
    back = back_piece(delta_table, full_weight)
    grad_field = grad_out + back.reshape(rows, lon_n, lev_n, chans)
    local_bias = jnp.sum(delta, axis=(0, 1, 2))
    local_land = jnp.sum(land_float[:, :, None, None] * delta, axis=(0, 1, 2))
    per_level = jnp.sum(grad_out * active, axis=(0, 1))
    local_gain = jnp.dot(one_hot.T, per_level, precision=highest)
    sums = all_sum(jnp.concatenate([local_bias[None], local_land[None], local_gain], axis=0))
    delta_flat = delta.reshape(-1, chans)
    grad_weight = lax.psum_scatter(
        stacked_product(delta_flat, table_pre), "space", scatter_dimension=1, tiled=True
    )
    grad_weight = jnp.transpose(grad_weight, (1, 0, 2))
    return (grad_field, grad_weight, sums[0], sums[1], sums[2 : 2 + local_gain.shape[0]])


def solution(mesh):
    in_specs = (
        P(("groups", "space"), None, None, None),
        P(("groups", "space"), None, None, None),
        P("space", None, None),
        P(),
        P(),
        P(),
        P("space", None),
        P(),
    )
    out_specs = (
        P(("groups", "space"), None, None, None),
        P(("groups", "space"), None, None),
        P("groups"),
        P("groups"),
        P("groups", None),
    )
    return jax.shard_map(
        per_device, mesh=mesh, in_specs=in_specs, out_specs=out_specs, check_vma=False
    )
```

profile of v0, /device:TPU:0, one launch (start us, length us, event | category | flops | bytes accessed | tf_op | source)
XLA Modules:
  0.0 206.0 jit_solution(803695057500846920)
XLA Ops:
  10.4 3.1 %collective-permute-start = (f32[1,40,8,256]{3,2,1,0:T(8,128)S(1)}, f32[1,40,8,256]{3,2,1,0:T(8,128)S(1)}, u32[]{:S(2)}, u32[]{:S(2)}) collective-permute-start(f32[1,40,8,256]{3,2,1,0:T(8,128)S(1)} %get-tuple-element.78), channel_id=1, source_target_pairs={{0,1},{1,2},{2,3},{3,4},{4,5},{5,6},{6,7},{7,8},{8,9},{9,10},{10,1... | collective-permute-start | bytes 983048 | tf_op jit(solution)/shard_map/ppermute | solution.py:17
  15.8 2.5 %pad_maximum_fusion.4 = (f32[2,40,8,256]{3,2,1,0:T(8,128)}, f32[4,40,8,256]{3,2,1,0:T(8,128)S(1)}, f32[2,40,8,256]{3,2,1,0:T(8,128)}) fusion(f32[1,40,8,256]{3,2,1,0:T(8,128)S(1)} %collective-permute-done.1, f32[2,40,8,256]{3,2,1,0:T(8,128)} %param.8, f32[4,40,8,256]{3,2,1,0:T(8,128)S(1)} %constant_dynamic-update-slice_fusion.2, ...), kind=kLoop, calls=%fused_computation.43 | loop fusion | flops 327680 | bytes 3276800 | tf_op jit(solution)/shard_map/concatenate | solution.py:19
  19.8 4.4 %fusion.25 = (f32[2,40,8,256]{3,2,1,0:T(8,128)}, f32[2,40,8,256]{3,2,1,0:T(8,128)}, f32[2,40,8,256]{3,2,1,0:T(8,128)}, f32[2,40,8,256]{3,2,1,0:T(8,128)}, f32[2,...) fusion(f32[4,42,10,256]{3,2,1,0:T(8,128)S(1)} %select_maximum_f, ...), kind=kLoop, calls=%fused_computation.122 | loop fusion | bytes 23592960 | tf_op jit(solution)/shard_map/slice | solution.py:38
  25.7 3.1 %pad_maximum_fusion.3 = (f32[2,40,8,256]{3,2,1,0:T(8,128)S(1)}, f32[2,40,8,256]{3,2,1,0:T(8,128)S(1)}, f32[2,40,8,256]{3,2,1,0:T(8,128)S(1)}, f32[2,40,8,256]{3,...) fusion(f32[4,1,8,256]{3,2,1,0:T(8,128)} %copy-done.36, f32[4,40,8,256]{3,2,1,0:T(8,128)} %copy-done.3, ...), kind=kLoop, calls=%fused_computation.42 | loop fusion | flops 983040 | bytes 5308416 | tf_op jit(solution)/shard_map/concatenate | solution.py:24
  38.0 6.6 %copy-done.2 = f32[640,27,256]{2,0,1:T(8,128)} copy-done((f32[640,27,256]{2,0,1:T(8,128)}, f32[640,27,256]{2,0,1:T(8,128)S(1)}, u32[]{:S(2)}) %copy-start.2) | copy-done | bytes 17694744
  44.6 7.4 %fusion.6 = (bf16[640,27,256]{2,0,1:T(8,128)(2,1)}, bf16[640,27,256]{2,0,1:T(8,128)(2,1)}) fusion(f32[640,27,256]{2,0,1:T(8,128)S(1)} %constant_dynamic-update-slice_fusion.3), kind=kLoop, calls=%fused_computation.8 | loop fusion | flops 17694720 | bytes 35389440 | tf_op jit(solution)/shard_map/convert_element_type | solution.py:74
  52.0 27.6 %all-gather.2.cloned.1.call-done = f32[256,27,256]{2,0,1:T(8,128)} async-done(((f32[16,27,256]{2,0,1:T(8,128)}), f32[256,27,256]{2,0,1:T(8,128)}) %all-gather.2.cloned.1.call-update) | async-done | bytes 7077904 | tf_op jit(solution)/shard_map/all_gather | solution.py:84
  79.6 13.7 %fusion.32 = f32[640,256,1]{1,0,2:T(8,128)S(1)} fusion(f32[640,27,256]{2,0,1:T(8,128)} %copy-done.2, f32[256,27,256]{2,0,1:T(8,128)} %all-gather.2.cloned.1.call-done), kind=kOutput, calls=%fused_computation.129 | convolution fusion | flops 6794772480 | bytes 25427968 | tf_op jit(solution)/shard_map/rop,poc->rc/dot_general | solution.py:46
  93.9 16.7 %fusion = f32[27,256,256]{2,1,0:T(8,128)} fusion(bf16[640,27,256]{2,0,1:T(8,128)(2,1)} %get-tuple-element.9, bf16[640,27,256]{2,0,1:T(8,128)(2,1)} %get-tuple-element.8, bf16[640,256]{1,0:T(8,128)(2,1)S(1)} %get-tuple-element.69, bf16[640,256]{1,0:T(8,128)(2,1)S(1)} %get-tuple-element.68), kind=kOutput, calls=%fused_computation | convolution fusion | flops 6877347840 | bytes 25427968 | tf_op jit(solution)/shard_map/rq,rop->opq/dot_general | solution.py:58
  111.3 2.2 %collective-permute-start.2 = (f32[1,40,8,256]{3,2,1,0:T(8,128)S(1)}, f32[1,40,8,256]{3,2,1,0:T(8,128)S(1)}, u32[]{:S(2)}, u32[]{:S(2)}) collective-permute-start(f32[1,40,8,256]{3,2,1,0:T(8,128)S(1)} %get-tuple-element.72), channel_id=1, source_target_pairs={{0,1},{1,2},{2,3},{3,4},{4,5},{5,6},{6,7},{7,8},{8,9},{9,10},{10,1... | collective-permute-start | bytes 983048 | tf_op jit(solution)/shard_map/ppermute | solution.py:17
  113.5 1.5 collective-permute-start.3
  115.0 2.7 %collective-permute-start.5 = (f32[6,256]{1,0:T(8,128)S(1)}, f32[6,256]{1,0:T(8,128)S(1)}, u32[]{:S(2)}, u32[]{:S(2)}) collective-permute-start(f32[6,256]{1,0:T(8,128)S(1)} %fusion.22), channel_id=1, source_target_pairs={{0,2},{1,3},{2,0},{3,1},{4,6},{5,7},{6,4},{7,5},{8,10},{9,11},{10,... | collective-permute-start | bytes 18440 | tf_op jit(solution)/shard_map/ppermute | solution.py:67
  117.7 4.9 %collective-permute-done.5 = f32[6,256]{1,0:T(8,128)S(1)} collective-permute-done((f32[6,256]{1,0:T(8,128)S(1)}, f32[6,256]{1,0:T(8,128)S(1)}, u32[]{:S(2)}, u32[]{:S(2)}) %collective-permute-start.5) | collective-permute-done | bytes 6176 | tf_op jit(solution)/shard_map/ppermute | solution.py:67
  122.6 2.9 %collective-permute-start.6 = (f32[6,256]{1,0:T(8,128)S(1)}, f32[6,256]{1,0:T(8,128)S(1)}, u32[]{:S(2)}, u32[]{:S(2)}) collective-permute-start(f32[6,256]{1,0:T(8,128)S(1)} %add.51), channel_id=1, source_target_pairs={{0,4},{1,5},{2,6},{3,7},{4,0},{5,1},{6,2},{7,3},{8,12},{9,13},{10,... | collective-permute-start | bytes 18440 | tf_op jit(solution)/shard_map/ppermute | solution.py:67
  125.5 1.6 collective-permute-done.6
  127.2 2.5 %collective-permute-start.7 = (f32[6,256]{1,0:T(8,128)S(1)}, f32[6,256]{1,0:T(8,128)S(1)}, u32[]{:S(2)}, u32[]{:S(2)}) collective-permute-start(f32[6,256]{1,0:T(8,128)S(1)} %add.52), channel_id=1, source_target_pairs={{0,8},{1,9},{2,10},{3,11},{4,12},{5,13},{6,14},{7,15},{8,0},{9,1},... | collective-permute-start | bytes 18440 | tf_op jit(solution)/shard_map/ppermute | solution.py:67
  129.7 2.0 collective-permute-done.7
  134.4 4.4 %fusion.24 = (f32[2,40,8,256]{3,2,1,0:T(8,128)}, f32[2,40,8,256]{3,2,1,0:T(8,128)}, f32[2,40,8,256]{3,2,1,0:T(8,128)}, f32[2,40,8,256]{3,2,1,0:T(8,128)}, f32[2,...) fusion(f32[4,42,10,256]{3,2,1,0:T(8,128)S(1)} %select_maximum_f, ...), kind=kLoop, calls=%fused_computation.121 | loop fusion | bytes 23592960 | tf_op jit(solution)/shard_map/slice | solution.py:38
  138.9 2.3 %constant_dynamic-update-slice_fusion.56 = f32[640,27,256]{2,0,1:T(8,128)} fusion(f32[640,1,256]{2,0,1:T(8,128)} %bitcast.118), kind=kLoop, calls=%fused_computation.107 | loop fusion | bytes 1310720
  141.1 1.9 maximum_maximum_fusion
  144.4 2.1 %constant_dynamic-update-slice_fusion.54 = f32[640,27,256]{2,0,1:T(8,128)} fusion(f32[640,27,256]{2,0,1:T(8,128)} %constant_dynamic-update-slice_fusion.55, f32[640,1,256]{2,0,1:T(8,128)} %bitcast.114), kind=kLoop, calls=%fused_computation.105 | loop fusion | bytes 1310720
  146.5 2.0 constant_dynamic-update-slice_fusion.53
  170.5 10.7 %fusion.33 = f32[640,256,1]{1,0,2:T(8,128)S(1)} fusion(f32[640,27,256]{2,0,1:T(8,128)} %constant_dynamic-update-slice_fusion.30, f32[256,27,256]{2,0,1:T(8,128)S(1)} %bitcast.79), kind=kOutput, calls=%fused_computation.130 | convolution fusion | flops 6794772480 | bytes 25427968 | tf_op jit(solution)/shard_map/roc,qoc->rq/dot_general | solution.py:50
  182.1 17.1 %reduce-scatter.2.cloned.1.call-done = f32[27,16,256]{2,1,0:T(8,128)} async-done(((f32[27,256,256]{2,1,0:T(8,128)}), f32[27,16,256]{2,1,0:T(8,128)}) %reduce-scatter.2.cloned.1.call-update) | async-done | bytes 442384 | tf_op jit(solution)/shard_map/reduce_scatter | solution.py:103
  (168 shorter events, 45.3 us)
Async XLA Ops:
  7.2 72.4 %all-gather.2.cloned.1.call-start = ((), (), s32[]{:S(2)}) async-start(), calls=%async_computation.1 | async-start | bytes 7520256 | tf_op jit(solution)/shard_map/all_gather | solution.py:84
  7.9 191.2 %reduce-scatter.2.cloned.1.call-start = ((), (), s32[]{:S(2)}) async-start(), calls=%async_computation.2 | async-start | bytes 7520256 | tf_op jit(solution)/shard_map/reduce_scatter | solution.py:103
  9.1 6.7 %collective-permute-start.1 = (f32[1,40,8,256]{3,2,1,0:T(8,128)S(1)}, f32[1,40,8,256]{3,2,1,0:T(8,128)S(1)}, u32[]{:S(2)}, u32[]{:S(2)}) collective-permute-start(f32[1,40,8,256]{3,2,1,0:T(8,128)S(1)} %get-tuple-element.77), channel_id=1, source_target_pairs={{1,0},{2,1},{3,2},{4,3},{5,4},{6,5},{7,6},{8,7},{9,8},{10,9},{11,1... | collective-permute-start | bytes 983048 | tf_op jit(solution)/shard_map/ppermute | solution.py:18
  10.4 5.4 %collective-permute-start = (f32[1,40,8,256]{3,2,1,0:T(8,128)S(1)}, f32[1,40,8,256]{3,2,1,0:T(8,128)S(1)}, u32[]{:S(2)}, u32[]{:S(2)}) collective-permute-start(f32[1,40,8,256]{3,2,1,0:T(8,128)S(1)} %get-tuple-element.78), channel_id=1, source_target_pairs={{0,1},{1,2},{2,3},{3,4},{4,5},{5,6},{6,7},{7,8},{8,9},{9,10},{10,1... | collective-permute-start | bytes 983048 | tf_op jit(solution)/shard_map/ppermute | solution.py:17
  52.0 41.4 %copy-start.33 = (f32[2,40,8,256]{3,2,1,0:T(8,128)S(1)}, f32[2,40,8,256]{3,2,1,0:T(8,128)}, u32[]{:S(2)}) copy-start(f32[2,40,8,256]{3,2,1,0:T(8,128)} %param.9) | copy-start | bytes 1966084
  52.0 41.4 %copy-start.37 = (f32[256]{0:T(256)S(1)}, f32[256]{0:T(256)}, u32[]{:S(2)}) copy-start(f32[256]{0:T(256)} %param.11) | copy-start | bytes 3076
  110.9 4.0 %collective-permute-start.4 = (f32[6,256]{1,0:T(8,128)S(1)}, f32[6,256]{1,0:T(8,128)S(1)}, u32[]{:S(2)}, u32[]{:S(2)}) collective-permute-start(f32[6,256]{1,0:T(8,128)S(1)} %pad_maximum_fusion.10), channel_id=1, source_target_pairs={{0,1},{1,0},{2,3},{3,2},{4,5},{5,4},{6,7},{7,6},{8,9},{9,8},{10,11... | collective-permute-start | bytes 18440 | tf_op jit(solution)/shard_map/ppermute | solution.py:67
  111.3 21.6 %collective-permute-start.2 = (f32[1,40,8,256]{3,2,1,0:T(8,128)S(1)}, f32[1,40,8,256]{3,2,1,0:T(8,128)S(1)}, u32[]{:S(2)}, u32[]{:S(2)}) collective-permute-start(f32[1,40,8,256]{3,2,1,0:T(8,128)S(1)} %get-tuple-element.72), channel_id=1, source_target_pairs={{0,1},{1,2},{2,3},{3,4},{4,5},{5,6},{6,7},{7,8},{8,9},{9,10},{10,1... | collective-permute-start | bytes 983048 | tf_op jit(solution)/shard_map/ppermute | solution.py:17
  113.5 19.4 %collective-permute-start.3 = (f32[1,40,8,256]{3,2,1,0:T(8,128)S(1)}, f32[1,40,8,256]{3,2,1,0:T(8,128)S(1)}, u32[]{:S(2)}, u32[]{:S(2)}) collective-permute-start(f32[1,40,8,256]{3,2,1,0:T(8,128)S(1)} %get-tuple-element.73), channel_id=1, source_target_pairs={{1,0},{2,1},{3,2},{4,3},{5,4},{6,5},{7,6},{8,7},{9,8},{10,9},{11,1... | collective-permute-start | bytes 983048 | tf_op jit(solution)/shard_map/ppermute | solution.py:18
  115.0 7.6 %collective-permute-start.5 = (f32[6,256]{1,0:T(8,128)S(1)}, f32[6,256]{1,0:T(8,128)S(1)}, u32[]{:S(2)}, u32[]{:S(2)}) collective-permute-start(f32[6,256]{1,0:T(8,128)S(1)} %fusion.22), channel_id=1, source_target_pairs={{0,2},{1,3},{2,0},{3,1},{4,6},{5,7},{6,4},{7,5},{8,10},{9,11},{10,... | collective-permute-start | bytes 18440 | tf_op jit(solution)/shard_map/ppermute | solution.py:67
  122.6 4.5 %collective-permute-start.6 = (f32[6,256]{1,0:T(8,128)S(1)}, f32[6,256]{1,0:T(8,128)S(1)}, u32[]{:S(2)}, u32[]{:S(2)}) collective-permute-start(f32[6,256]{1,0:T(8,128)S(1)} %add.51), channel_id=1, source_target_pairs={{0,4},{1,5},{2,6},{3,7},{4,0},{5,1},{6,2},{7,3},{8,12},{9,13},{10,... | collective-permute-start | bytes 18440 | tf_op jit(solution)/shard_map/ppermute | solution.py:67
  127.2 4.5 %collective-permute-start.7 = (f32[6,256]{1,0:T(8,128)S(1)}, f32[6,256]{1,0:T(8,128)S(1)}, u32[]{:S(2)}, u32[]{:S(2)}) collective-permute-start(f32[6,256]{1,0:T(8,128)S(1)} %add.52), channel_id=1, source_target_pairs={{0,8},{1,9},{2,10},{3,11},{4,12},{5,13},{6,14},{7,15},{8,0},{9,1},... | collective-permute-start | bytes 18440 | tf_op jit(solution)/shard_map/ppermute | solution.py:67
  138.8 18.1 %copy-start.23 = (f32[2,40,8,256]{3,2,1,0:T(8,128)S(1)}, f32[2,40,8,256]{3,2,1,0:T(8,128)}, u32[]{:S(2)}) copy-start(f32[2,40,8,256]{3,2,1,0:T(8,128)} %get-tuple-element.19) | copy-start | bytes 1966084
  138.8 20.0 %copy-start.20 = (f32[2,40,8,256]{3,2,1,0:T(8,128)S(1)}, f32[2,40,8,256]{3,2,1,0:T(8,128)}, u32[]{:S(2)}) copy-start(f32[2,40,8,256]{3,2,1,0:T(8,128)} %get-tuple-element.18) | copy-start | bytes 1966084
  138.9 20.9 %copy-start.19 = (f32[2,40,8,256]{3,2,1,0:T(8,128)S(1)}, f32[2,40,8,256]{3,2,1,0:T(8,128)}, u32[]{:S(2)}) copy-start(f32[2,40,8,256]{3,2,1,0:T(8,128)} %get-tuple-element.17) | copy-start | bytes 1966084
  141.1 20.4 %copy-start.16 = (f32[2,40,8,256]{3,2,1,0:T(8,128)S(1)}, f32[2,40,8,256]{3,2,1,0:T(8,128)}, u32[]{:S(2)}) copy-start(f32[2,40,8,256]{3,2,1,0:T(8,128)} %get-tuple-element.16) | copy-start | bytes 1966084
  141.1 21.3 %copy-start.15 = (f32[2,40,8,256]{3,2,1,0:T(8,128)S(1)}, f32[2,40,8,256]{3,2,1,0:T(8,128)}, u32[]{:S(2)}) copy-start(f32[2,40,8,256]{3,2,1,0:T(8,128)} %get-tuple-element.15) | copy-start | bytes 1966084
  143.1 21.1 %copy-start.12 = (f32[2,40,8,256]{3,2,1,0:T(8,128)S(1)}, f32[2,40,8,256]{3,2,1,0:T(8,128)}, u32[]{:S(2)}) copy-start(f32[2,40,8,256]{3,2,1,0:T(8,128)} %get-tuple-element.14) | copy-start | bytes 1966084
  143.1 22.0 %copy-start.11 = (f32[2,40,8,256]{3,2,1,0:T(8,128)S(1)}, f32[2,40,8,256]{3,2,1,0:T(8,128)}, u32[]{:S(2)}) copy-start(f32[2,40,8,256]{3,2,1,0:T(8,128)} %get-tuple-element.13) | copy-start | bytes 1966084
  143.5 23.4 %copy-start.9 = (f32[2,40,8,256]{3,2,1,0:T(8,128)S(1)}, f32[2,40,8,256]{3,2,1,0:T(8,128)}, u32[]{:S(2)}) copy-start(f32[2,40,8,256]{3,2,1,0:T(8,128)} %get-tuple-element.12) | copy-start | bytes 1966084
  143.5 24.3 %copy-start.8 = (f32[2,40,8,256]{3,2,1,0:T(8,128)S(1)}, f32[2,40,8,256]{3,2,1,0:T(8,128)}, u32[]{:S(2)}) copy-start(f32[2,40,8,256]{3,2,1,0:T(8,128)} %get-tuple-element.11) | copy-start | bytes 1966084
  143.5 26.1 %copy-start.7 = (f32[2,40,8,256]{3,2,1,0:T(8,128)S(1)}, f32[2,40,8,256]{3,2,1,0:T(8,128)}, u32[]{:S(2)}) copy-start(f32[2,40,8,256]{3,2,1,0:T(8,128)} %get-tuple-element.10) | copy-start | bytes 1966084
  144.4 26.1 %slice-start = ((s8[7077888]{0:T(1024)(128)(4,1)}), s8[4194304]{0:T(1024)(128)(4,1)S(1)}, s32[]{:S(2)}) async-start(s8[7077888]{0:T(1024)(128)(4,1)} %bitcast.78), calls=%async_computation.3 | async-start | bytes 8388608
  166.9 32.3 %copy-start.1 = (f32[4,256]{1,0:T(4,128)S(1)}, f32[4,256]{1,0:T(4,128)}, u32[]{:S(2)}) copy-start(f32[4,256]{1,0:T(4,128)} %param.13) | copy-start | bytes 12292
  (27 other events, 303.6 us)
Sparse Core Ops, SparseCore 0:
  10.2 69.3 all-gather.1
  110.7 88.3 reduce-scatter.1
where the time goes:
time: 207 us; the launch traced here: 206 us
  local copies, waits for them, and re-layouts  58.4 us (28%)
  waiting for transfers between devices  54 us (26%)
  matrix products  42.2 us (20%)
  other arithmetic  20.1 us (10%)
  starting transfers between devices  16.6 us (8%)
  between operations  14.8 us (7%)
    unnamed x135, local copies, waits for them, and re-layouts  45.8 us
    all_gather x1, waiting for transfers between devices, per_device(): full_weight = lax.all_gather(weight, 'space', axis=0, tiled=True)  27.6 us
    reduce_scatter x1, waiting for transfers between devices, per_device(): lax.psum_scatter(stacked_product(delta_flat, table_pre), 'space', scatter...  17.1 us
    dot_general x1, matrix products, stacked_product(): jnp.einsum('rq,rop->opq', lhs, rhs, preferred_element_type=jnp.float32)  16.7 us
    dot_general x1, matrix products, conv_piece(): return jnp.einsum('rop,poc->rc', table, piece, precision=high)  13.7 us
    dot_general x1, matrix products, back_piece(): return jnp.einsum('roc,qoc->rq', table, piece, precision=high)  10.7 us
    slice x3, local copies, waits for them, and re-layouts, window_table(): grid[lat_off:lat_off + out_rows, lon_off:lon_off + lon_n, lev_off:lev_off...  9.24 us
    ppermute x4, waiting for transfers between devices, all_sum(): x = x + lax.ppermute(x, 'space', [(i, i ^ bit) for i in range(count)])  8.57 us
  transfers between devices with their start and end apart: 10, of which 5 were waited for; matrix products, arithmetic and copies ran while one was open for 39% of the time, Pallas kernels for 0%

commit v1 on v0

--- a/solution.py
+++ b/solution.py
@@ -81,7 +81,14 @@
         level_index[:, None] == jnp.arange(level_gain.shape[0], dtype=jnp.int32)[None, :]
     ).astype(jnp.float32)
     gains = jnp.dot(one_hot, level_gain, precision=highest)
-    full_weight = lax.all_gather(weight, "space", axis=0, tiled=True)
+    ring = [weight]
+    for hop in range(15):
+        ring.append(lax.ppermute(ring[-1], "space", [(dev, (dev + 1) % 16) for dev in range(16)]))
+    full_weight = jnp.roll(
+        jnp.concatenate(ring[::-1], axis=0),
+        (lax.axis_index("space") + 1) * ring[0].shape[0],
+        axis=0,
+    )
     grid_pre = wrap_levels(with_halo(field, (("space", 0),), 1))
     table_pre = window_table(grid_pre, rows, False)
     conv = conv_piece(table_pre, full_weight)

time: 207 us -> 312 us (1.51)
  waiting for transfers between devices: 54 us -> 156 us
  starting transfers between devices: 16.6 us -> 11.7 us
  local copies, waits for them, and re-layouts: 58.4 us -> 61.6 us
    ppermute x0 -> x15, waiting for transfers between devices: none -> 123 us  [per_device(): lax.ppermute(ring[-1], 'space', [(dev, (dev + 1) % 16) for dev in range(1...]
    all_gather x1 -> x0, waiting for transfers between devices: 27.6 us -> none  [per_device(): full_weight = lax.all_gather(weight, 'space', axis=0, tiled=True)]
    ppermute x4, starting transfers between devices: 8.5 us -> 2.84 us  [all_sum(): x = x + lax.ppermute(x, 'space', [(i, i ^ bit) for i in range(count)])]
    ppermute x4, waiting for transfers between devices: 8.57 us -> 12.6 us  [all_sum(): x = x + lax.ppermute(x, 'space', [(i, i ^ bit) for i in range(count)])]
    unnamed x135 -> x228, local copies, waits for them, and re-layouts: 45.8 us -> 49.4 us
    reduce_scatter x1, waiting for transfers between devices: 17.1 us -> 20.4 us  [per_device(): lax.psum_scatter(stacked_product(delta_flat, table_pre), 'space', scatter...]
  transfers between devices with their start and end apart: 10 -> 24, of which waited for: 5 -> 19; matrix products, arithmetic and copies ran while one was open for 39% -> 25% of each run, Pallas kernels for 0% -> 0%
where the time goes in v1:
time: 312 us; the launch traced here: 311 us
  waiting for transfers between devices  156 us (50%)
  local copies, waits for them, and re-layouts  61.6 us (20%)
  matrix products  44.5 us (14%)
  other arithmetic  21.7 us (7%)
  between operations  15.3 us (5%)
  starting transfers between devices  11.7 us (4%)
    ppermute x15, waiting for transfers between devices, per_device(): lax.ppermute(ring[-1], 'space', [(dev, (dev + 1) % 16) for dev in range(1...  123 us
    unnamed x228, local copies, waits for them, and re-layouts  49.4 us
    reduce_scatter x1, waiting for transfers between devices, per_device(): lax.psum_scatter(stacked_product(delta_flat, table_pre), 'space', scatter...  20.4 us
    dot_general x1, matrix products, stacked_product(): jnp.einsum('rq,rop->opq', lhs, rhs, preferred_element_type=jnp.float32)  16.2 us
    dot_general x1, matrix products, conv_piece(): return jnp.einsum('rop,poc->rc', table, piece, precision=high)  15.8 us
    ppermute x4, waiting for transfers between devices, all_sum(): x = x + lax.ppermute(x, 'space', [(i, i ^ bit) for i in range(count)])  12.6 us
    dot_general x1, matrix products, back_piece(): return jnp.einsum('roc,qoc->rq', table, piece, precision=high)  11.5 us
    slice x3, local copies, waits for them, and re-layouts, window_table(): grid[lat_off:lat_off + out_rows, lon_off:lon_off + lon_n, lev_off:lev_off...  8.92 us
  transfers between devices with their start and end apart: 24, of which 19 were waited for; matrix products, arithmetic and copies ran while one was open for 25% of the time, Pallas kernels for 0%

profile of v1, /device:TPU:0, one launch (start us, length us, event | category | flops | bytes accessed | tf_op | source)
XLA Modules:
  0.0 311.3 jit_solution(8129849673148904378)
XLA Ops:
  7.7 11.2 %collective-permute-done.2 = f32[16,27,256]{2,0,1:T(8,128)S(1)} collective-permute-done((f32[16,27,256]{2,0,1:T(8,128)}, f32[16,27,256]{2,0,1:T(8,128)S(1)}, u32[]{:S(2)}, u32[]{:S(2)}) %collective-permute-start.2) | collective-permute-done | bytes 442400 | tf_op jit(solution)/shard_map/ppermute | solution.py:86
  19.7 10.4 %collective-permute-done.3 = f32[16,27,256]{2,0,1:T(8,128)S(1)} collective-permute-done((f32[16,27,256]{2,0,1:T(8,128)S(1)}, f32[16,27,256]{2,0,1:T(8,128)S(1)}, u32[]{:S(2)}, u32[]{:S(2)}) %collective-permute-start.3) | collective-permute-done | bytes 442400 | tf_op jit(solution)/shard_map/ppermute | solution.py:86
  30.9 10.4 %collective-permute-done.4 = f32[16,27,256]{2,0,1:T(8,128)S(1)} collective-permute-done((f32[16,27,256]{2,0,1:T(8,128)S(1)}, f32[16,27,256]{2,0,1:T(8,128)S(1)}, u32[]{:S(2)}, u32[]{:S(2)}) %collective-permute-start.4) | collective-permute-done | bytes 442400 | tf_op jit(solution)/shard_map/ppermute | solution.py:86
  44.5 3.1 collective-permute-start
  56.0 6.9 %collective-permute-done.6 = f32[16,27,256]{2,0,1:T(8,128)S(1)} collective-permute-done((f32[16,27,256]{2,0,1:T(8,128)S(1)}, f32[16,27,256]{2,0,1:T(8,128)S(1)}, u32[]{:S(2)}, u32[]{:S(2)}) %collective-permute-start.6) | collective-permute-done | bytes 442400 | tf_op jit(solution)/shard_map/ppermute | solution.py:86
  63.4 10.0 %collective-permute-done.7 = f32[16,27,256]{2,0,1:T(8,128)} collective-permute-done((f32[16,27,256]{2,0,1:T(8,128)S(1)}, f32[16,27,256]{2,0,1:T(8,128)}, u32[]{:S(2)}, u32[]{:S(2)}) %collective-permute-start.7) | collective-permute-done | bytes 442400 | tf_op jit(solution)/shard_map/ppermute | solution.py:86
  73.5 4.2 %fusion.31 = (f32[2,40,8,256]{3,2,1,0:T(8,128)S(1)}, f32[2,40,8,256]{3,2,1,0:T(8,128)}, f32[2,40,8,256]{3,2,1,0:T(8,128)}, f32[2,40,8,256]{3,2,1,0:T(8,128)}, f3...) fusion(f32[4,42,10,256]{3,2,1,0:T(8,128)S(1)} %select_maximum_f, ...), kind=kLoop, calls=%fused_computation.160 | loop fusion | bytes 23592960 | tf_op jit(solution)/shard_map/slice | solution.py:38
  79.0 5.2 %collective-permute-done.8 = f32[16,27,256]{2,0,1:T(8,128)} collective-permute-done((f32[16,27,256]{2,0,1:T(8,128)}, f32[16,27,256]{2,0,1:T(8,128)}, u32[]{:S(2)}, u32[]{:S(2)}) %collective-permute-start.8) | collective-permute-done | bytes 442400 | tf_op jit(solution)/shard_map/ppermute | solution.py:86
  88.1 6.8 %collective-permute-done.9 = f32[16,27,256]{2,0,1:T(8,128)S(1)} collective-permute-done((f32[16,27,256]{2,0,1:T(8,128)}, f32[16,27,256]{2,0,1:T(8,128)S(1)}, u32[]{:S(2)}, u32[]{:S(2)}) %collective-permute-start.9) | collective-permute-done | bytes 442400 | tf_op jit(solution)/shard_map/ppermute | solution.py:86
  99.6 5.7 %collective-permute-done.10 = f32[16,27,256]{2,0,1:T(8,128)S(1)} collective-permute-done((f32[16,27,256]{2,0,1:T(8,128)S(1)}, f32[16,27,256]{2,0,1:T(8,128)S(1)}, u32[]{:S(2)}, u32[]{:S(2)}) %collective-permute-start.10) | collective-permute-done | bytes 442400 | tf_op jit(solution)/shard_map/ppermute | solution.py:86
  105.5 10.2 %collective-permute-done.11 = f32[16,27,256]{2,0,1:T(8,128)S(1)} collective-permute-done((f32[16,27,256]{2,0,1:T(8,128)S(1)}, f32[16,27,256]{2,0,1:T(8,128)S(1)}, u32[]{:S(2)}, u32[]{:S(2)}) %collective-permute-start.11) | collective-permute-done | bytes 442400 | tf_op jit(solution)/shard_map/ppermute | solution.py:86
  116.0 10.2 %collective-permute-done.12 = f32[16,27,256]{2,0,1:T(8,128)S(1)} collective-permute-done((f32[16,27,256]{2,0,1:T(8,128)S(1)}, f32[16,27,256]{2,0,1:T(8,128)S(1)}, u32[]{:S(2)}, u32[]{:S(2)}) %collective-permute-start.12) | collective-permute-done | bytes 442400 | tf_op jit(solution)/shard_map/ppermute | solution.py:86
  126.4 10.2 %collective-permute-done.13 = f32[16,27,256]{2,0,1:T(8,128)S(1)} collective-permute-done((f32[16,27,256]{2,0,1:T(8,128)S(1)}, f32[16,27,256]{2,0,1:T(8,128)S(1)}, u32[]{:S(2)}, u32[]{:S(2)}) %collective-permute-start.13) | collective-permute-done | bytes 442400 | tf_op jit(solution)/shard_map/ppermute | solution.py:86
  136.8 10.2 %collective-permute-done.14 = f32[16,27,256]{2,0,1:T(8,128)S(1)} collective-permute-done((f32[16,27,256]{2,0,1:T(8,128)S(1)}, f32[16,27,256]{2,0,1:T(8,128)S(1)}, u32[]{:S(2)}, u32[]{:S(2)}) %collective-permute-start.14) | collective-permute-done | bytes 442400 | tf_op jit(solution)/shard_map/ppermute | solution.py:86
  147.3 10.1 %collective-permute-done.15 = f32[16,27,256]{2,0,1:T(8,128)S(1)} collective-permute-done((f32[16,27,256]{2,0,1:T(8,128)S(1)}, f32[16,27,256]{2,0,1:T(8,128)S(1)}, u32[]{:S(2)}, u32[]{:S(2)}) %collective-permute-start.15) | collective-permute-done | bytes 442400 | tf_op jit(solution)/shard_map/ppermute | solution.py:86
  157.4 7.4 %fusion.6 = (bf16[640,27,256]{2,0,1:T(8,128)(2,1)}, bf16[640,27,256]{2,0,1:T(8,128)(2,1)}) fusion(f32[640,27,256]{2,0,1:T(8,128)S(1)} %constant_dynamic-update-slice_fusion.3), kind=kLoop, calls=%fused_computation.8 | loop fusion | flops 17694720 | bytes 35389440 | tf_op jit(solution)/shard_map/convert_element_type | solution.py:74
  181.6 15.8 %fusion.9 = f32[640,256,1]{1,0,2:T(8,128)} fusion(f32[640,27,256]{2,0,1:T(8,128)} %copy-done.2, f32[512,27,256]{2,0,1:T(8,128)S(1)} %constant_dynamic-update-slice_fusion.30, s32[]{:T(128)S(6)} %select_n.14), kind=kOutput, calls=%fused_computation.11 | convolution fusion | flops 6794772480 | bytes 25427972 | tf_op jit(solution)/shard_map/rop,poc->rc/dot_general | solution.py:46
  199.2 16.2 %fusion = f32[27,256,256]{2,1,0:T(8,128)} fusion(bf16[640,27,256]{2,0,1:T(8,128)(2,1)} %get-tuple-element.9, bf16[640,27,256]{2,0,1:T(8,128)(2,1)} %get-tuple-element.8, bf16[640,256]{1,0:T(8,128)(2,1)S(1)} %get-tuple-element.69, bf16[640,256]{1,0:T(8,128)(2,1)S(1)} %get-tuple-element.68), kind=kOutput, calls=%fused_computation | convolution fusion | flops 6877347840 | bytes 25427968 | tf_op jit(solution)/shard_map/rq,rop->opq/dot_general | solution.py:58
  222.1 4.9 %collective-permute-done.20 = f32[6,256]{1,0:T(8,128)S(1)} collective-permute-done((f32[6,256]{1,0:T(8,128)S(1)}, f32[6,256]{1,0:T(8,128)S(1)}, u32[]{:S(2)}, u32[]{:S(2)}) %collective-permute-start.20) | collective-permute-done | bytes 6176 | tf_op jit(solution)/shard_map/ppermute | solution.py:67
  227.0 3.6 %collective-permute-done.21 = f32[6,256]{1,0:T(8,128)S(1)} collective-permute-done((f32[6,256]{1,0:T(8,128)S(1)}, f32[6,256]{1,0:T(8,128)S(1)}, u32[]{:S(2)}, u32[]{:S(2)}) %collective-permute-start.21) | collective-permute-done | bytes 6176 | tf_op jit(solution)/shard_map/ppermute | solution.py:67
  231.1 4.1 %collective-permute-done.22 = f32[6,256]{1,0:T(8,128)S(1)} collective-permute-done((f32[6,256]{1,0:T(8,128)S(1)}, f32[6,256]{1,0:T(8,128)S(1)}, u32[]{:S(2)}, u32[]{:S(2)}) %collective-permute-start.22) | collective-permute-done | bytes 6176 | tf_op jit(solution)/shard_map/ppermute | solution.py:67
  237.8 4.4 %fusion.30 = (f32[2,40,8,256]{3,2,1,0:T(8,128)}, f32[2,40,8,256]{3,2,1,0:T(8,128)}, f32[2,40,8,256]{3,2,1,0:T(8,128)}, f32[2,40,8,256]{3,2,1,0:T(8,128)}, f32[2,...) fusion(f32[4,42,10,256]{3,2,1,0:T(8,128)S(1)} %select_maximum_f, ...), kind=kLoop, calls=%fused_computation.159 | loop fusion | bytes 23592960 | tf_op jit(solution)/shard_map/slice | solution.py:38
  270.3 11.5 %fusion.7 = f32[640,256,1]{1,0,2:T(8,128)} fusion(f32[640,27,256]{2,0,1:T(8,128)} %constant_dynamic-update-slice_fusion.62, f32[512,27,256]{2,0,1:T(8,128)S(1)} %bitcast.77, s32[]{:T(128)S(6)} %select_n.14), kind=kOutput, calls=%fused_computation.9 | convolution fusion | flops 6794772480 | bytes 25427972 | tf_op jit(solution)/shard_map/roc,qoc->rq/dot_general | solution.py:50
  284.0 20.4 %reduce-scatter.2.cloned.1.call-done = f32[27,16,256]{2,1,0:T(8,128)} async-done(((f32[27,256,256]{2,1,0:T(8,128)}), f32[27,16,256]{2,1,0:T(8,128)}) %reduce-scatter.2.cloned.1.call-update) | async-done | bytes 442384 | tf_op jit(solution)/shard_map/reduce_scatter | solution.py:110
  (289 shorter events, 83.0 us)
Async XLA Ops:
  7.2 297.2 %reduce-scatter.2.cloned.1.call-start = ((), (), s32[]{:S(2)}) async-start(), calls=%async_computation.1 | async-start | bytes 7520256 | tf_op jit(solution)/shard_map/reduce_scatter | solution.py:110
  7.2 11.7 %collective-permute-start.2 = (f32[16,27,256]{2,0,1:T(8,128)}, f32[16,27,256]{2,0,1:T(8,128)S(1)}, u32[]{:S(2)}, u32[]{:S(2)}) collective-permute-start(f32[16,27,256]{2,0,1:T(8,128)} %param.10), channel_id=1, source_target_pairs={{0,1},{1,2},{2,3},{3,4},{4,5},{5,6},{6,7},{7,8},{8,9},{9,10},{10,1... | collective-permute-start | bytes 1327112 | tf_op jit(solution)/shard_map/ppermute | solution.py:86
  19.7 10.4 %collective-permute-start.3 = (f32[16,27,256]{2,0,1:T(8,128)S(1)}, f32[16,27,256]{2,0,1:T(8,128)S(1)}, u32[]{:S(2)}, u32[]{:S(2)}) collective-permute-start(f32[16,27,256]{2,0,1:T(8,128)S(1)} %collective-permute-done.2), channel_id=1, source_target_pairs={{0,1},{1,2},{2,3},{3,4},{4,5},{5,6},{6,7},{7,8},{8,9},{9,10},{10,1... | collective-permute-start | bytes 1327112 | tf_op jit(solution)/shard_map/ppermute | solution.py:86
  30.9 10.4 %collective-permute-start.4 = (f32[16,27,256]{2,0,1:T(8,128)S(1)}, f32[16,27,256]{2,0,1:T(8,128)S(1)}, u32[]{:S(2)}, u32[]{:S(2)}) collective-permute-start(f32[16,27,256]{2,0,1:T(8,128)S(1)} %collective-permute-done.3), channel_id=1, source_target_pairs={{0,1},{1,2},{2,3},{3,4},{4,5},{5,6},{6,7},{7,8},{8,9},{9,10},{10,1... | collective-permute-start | bytes 1327112 | tf_op jit(solution)/shard_map/ppermute | solution.py:86
  42.1 10.4 %collective-permute-start.5 = (f32[16,27,256]{2,0,1:T(8,128)S(1)}, f32[16,27,256]{2,0,1:T(8,128)S(1)}, u32[]{:S(2)}, u32[]{:S(2)}) collective-permute-start(f32[16,27,256]{2,0,1:T(8,128)S(1)} %collective-permute-done.4), channel_id=1, source_target_pairs={{0,1},{1,2},{2,3},{3,4},{4,5},{5,6},{6,7},{7,8},{8,9},{9,10},{10,1... | collective-permute-start | bytes 1327112 | tf_op jit(solution)/shard_map/ppermute | solution.py:86
  43.2 10.2 %collective-permute-start.1 = (f32[1,40,8,256]{3,2,1,0:T(8,128)S(1)}, f32[1,40,8,256]{3,2,1,0:T(8,128)S(1)}, u32[]{:S(2)}, u32[]{:S(2)}) collective-permute-start(f32[1,40,8,256]{3,2,1,0:T(8,128)S(1)} %get-tuple-element.77), channel_id=1, source_target_pairs={{1,0},{2,1},{3,2},{4,3},{5,4},{6,5},{7,6},{8,7},{9,8},{10,9},{11,1... | collective-permute-start | bytes 983048 | tf_op jit(solution)/shard_map/ppermute | solution.py:18
  44.5 8.9 %collective-permute-start = (f32[1,40,8,256]{3,2,1,0:T(8,128)S(1)}, f32[1,40,8,256]{3,2,1,0:T(8,128)S(1)}, u32[]{:S(2)}, u32[]{:S(2)}) collective-permute-start(f32[1,40,8,256]{3,2,1,0:T(8,128)S(1)} %get-tuple-element.78), channel_id=1, source_target_pairs={{0,1},{1,2},{2,3},{3,4},{4,5},{5,6},{6,7},{7,8},{8,9},{9,10},{10,1... | collective-permute-start | bytes 983048 | tf_op jit(solution)/shard_map/ppermute | solution.py:17
  52.5 10.4 %collective-permute-start.6 = (f32[16,27,256]{2,0,1:T(8,128)S(1)}, f32[16,27,256]{2,0,1:T(8,128)S(1)}, u32[]{:S(2)}, u32[]{:S(2)}) collective-permute-start(f32[16,27,256]{2,0,1:T(8,128)S(1)} %collective-permute-done.5), channel_id=1, source_target_pairs={{0,1},{1,2},{2,3},{3,4},{4,5},{5,6},{6,7},{7,8},{8,9},{9,10},{10,1... | collective-permute-start | bytes 1327112 | tf_op jit(solution)/shard_map/ppermute | solution.py:86
  63.0 10.5 %collective-permute-start.7 = (f32[16,27,256]{2,0,1:T(8,128)S(1)}, f32[16,27,256]{2,0,1:T(8,128)}, u32[]{:S(2)}, u32[]{:S(2)}) collective-permute-start(f32[16,27,256]{2,0,1:T(8,128)S(1)} %collective-permute-done.6), channel_id=1, source_target_pairs={{0,1},{1,2},{2,3},{3,4},{4,5},{5,6},{6,7},{7,8},{8,9},{9,10},{10,1... | collective-permute-start | bytes 1327112 | tf_op jit(solution)/shard_map/ppermute | solution.py:86
  73.5 10.7 %collective-permute-start.8 = (f32[16,27,256]{2,0,1:T(8,128)}, f32[16,27,256]{2,0,1:T(8,128)}, u32[]{:S(2)}, u32[]{:S(2)}) collective-permute-start(f32[16,27,256]{2,0,1:T(8,128)} %collective-permute-done.7), channel_id=1, source_target_pairs={{0,1},{1,2},{2,3},{3,4},{4,5},{5,6},{6,7},{7,8},{8,9},{9,10},{10,1... | collective-permute-start | bytes 1327112 | tf_op jit(solution)/shard_map/ppermute | solution.py:86
  84.2 10.6 %collective-permute-start.9 = (f32[16,27,256]{2,0,1:T(8,128)}, f32[16,27,256]{2,0,1:T(8,128)S(1)}, u32[]{:S(2)}, u32[]{:S(2)}) collective-permute-start(f32[16,27,256]{2,0,1:T(8,128)} %collective-permute-done.8), channel_id=1, source_target_pairs={{0,1},{1,2},{2,3},{3,4},{4,5},{5,6},{6,7},{7,8},{8,9},{9,10},{10,1... | collective-permute-start | bytes 1327112 | tf_op jit(solution)/shard_map/ppermute | solution.py:86
  94.9 10.4 %collective-permute-start.10 = (f32[16,27,256]{2,0,1:T(8,128)S(1)}, f32[16,27,256]{2,0,1:T(8,128)S(1)}, u32[]{:S(2)}, u32[]{:S(2)}) collective-permute-start(f32[16,27,256]{2,0,1:T(8,128)S(1)} %collective-permute-done.9), channel_id=1, source_target_pairs={{0,1},{1,2},{2,3},{3,4},{4,5},{5,6},{6,7},{7,8},{8,9},{9,10},{10,1... | collective-permute-start | bytes 1327112 | tf_op jit(solution)/shard_map/ppermute | solution.py:86
  105.3 10.4 %collective-permute-start.11 = (f32[16,27,256]{2,0,1:T(8,128)S(1)}, f32[16,27,256]{2,0,1:T(8,128)S(1)}, u32[]{:S(2)}, u32[]{:S(2)}) collective-permute-start(f32[16,27,256]{2,0,1:T(8,128)S(1)} %collective-permute-done.10), channel_id=1, source_target_pairs={{0,1},{1,2},{2,3},{3,4},{4,5},{5,6},{6,7},{7,8},{8,9},{9,10},{10,1... | collective-permute-start | bytes 1327112 | tf_op jit(solution)/shard_map/ppermute | solution.py:86
  115.7 10.4 %collective-permute-start.12 = (f32[16,27,256]{2,0,1:T(8,128)S(1)}, f32[16,27,256]{2,0,1:T(8,128)S(1)}, u32[]{:S(2)}, u32[]{:S(2)}) collective-permute-start(f32[16,27,256]{2,0,1:T(8,128)S(1)} %collective-permute-done.11), channel_id=1, source_target_pairs={{0,1},{1,2},{2,3},{3,4},{4,5},{5,6},{6,7},{7,8},{8,9},{9,10},{10,1... | collective-permute-start | bytes 1327112 | tf_op jit(solution)/shard_map/ppermute | solution.py:86
  126.1 10.4 %collective-permute-start.13 = (f32[16,27,256]{2,0,1:T(8,128)S(1)}, f32[16,27,256]{2,0,1:T(8,128)S(1)}, u32[]{:S(2)}, u32[]{:S(2)}) collective-permute-start(f32[16,27,256]{2,0,1:T(8,128)S(1)} %collective-permute-done.12), channel_id=1, source_target_pairs={{0,1},{1,2},{2,3},{3,4},{4,5},{5,6},{6,7},{7,8},{8,9},{9,10},{10,1... | collective-permute-start | bytes 1327112 | tf_op jit(solution)/shard_map/ppermute | solution.py:86
  136.6 10.4 %collective-permute-start.14 = (f32[16,27,256]{2,0,1:T(8,128)S(1)}, f32[16,27,256]{2,0,1:T(8,128)S(1)}, u32[]{:S(2)}, u32[]{:S(2)}) collective-permute-start(f32[16,27,256]{2,0,1:T(8,128)S(1)} %collective-permute-done.13), channel_id=1, source_target_pairs={{0,1},{1,2},{2,3},{3,4},{4,5},{5,6},{6,7},{7,8},{8,9},{9,10},{10,1... | collective-permute-start | bytes 1327112 | tf_op jit(solution)/shard_map/ppermute | solution.py:86
  147.0 10.4 %collective-permute-start.15 = (f32[16,27,256]{2,0,1:T(8,128)S(1)}, f32[16,27,256]{2,0,1:T(8,128)S(1)}, u32[]{:S(2)}, u32[]{:S(2)}) collective-permute-start(f32[16,27,256]{2,0,1:T(8,128)S(1)} %collective-permute-done.14), channel_id=1, source_target_pairs={{0,1},{1,2},{2,3},{3,4},{4,5},{5,6},{6,7},{7,8},{8,9},{9,10},{10,1... | collective-permute-start | bytes 1327112 | tf_op jit(solution)/shard_map/ppermute | solution.py:86
  157.4 10.5 %collective-permute-start.16 = (f32[16,27,256]{2,0,1:T(8,128)S(1)}, f32[16,27,256]{2,0,1:T(8,128)}, u32[]{:S(2)}, u32[]{:S(2)}) collective-permute-start(f32[16,27,256]{2,0,1:T(8,128)S(1)} %collective-permute-done.15), channel_id=1, source_target_pairs={{0,1},{1,2},{2,3},{3,4},{4,5},{5,6},{6,7},{7,8},{8,9},{9,10},{10,1... | collective-permute-start | bytes 1327112 | tf_op jit(solution)/shard_map/ppermute | solution.py:86
  215.7 4.1 %collective-permute-start.19 = (f32[6,256]{1,0:T(8,128)S(1)}, f32[6,256]{1,0:T(8,128)S(1)}, u32[]{:S(2)}, u32[]{:S(2)}) collective-permute-start(f32[6,256]{1,0:T(8,128)S(1)} %pad_maximum_fusion.10), channel_id=1, source_target_pairs={{0,1},{1,0},{2,3},{3,2},{4,5},{5,4},{6,7},{7,6},{8,9},{9,8},{10,11... | collective-permute-start | bytes 18440 | tf_op jit(solution)/shard_map/ppermute | solution.py:67
  215.9 20.6 %collective-permute-start.17 = (f32[1,40,8,256]{3,2,1,0:T(8,128)S(1)}, f32[1,40,8,256]{3,2,1,0:T(8,128)S(1)}, u32[]{:S(2)}, u32[]{:S(2)}) collective-permute-start(f32[1,40,8,256]{3,2,1,0:T(8,128)S(1)} %get-tuple-element.72), channel_id=1, source_target_pairs={{0,1},{1,2},{2,3},{3,4},{4,5},{5,6},{6,7},{7,8},{8,9},{9,10},{10,1... | collective-permute-start | bytes 983048 | tf_op jit(solution)/shard_map/ppermute | solution.py:17
  218.3 18.1 %collective-permute-start.18 = (f32[1,40,8,256]{3,2,1,0:T(8,128)S(1)}, f32[1,40,8,256]{3,2,1,0:T(8,128)S(1)}, u32[]{:S(2)}, u32[]{:S(2)}) collective-permute-start(f32[1,40,8,256]{3,2,1,0:T(8,128)S(1)} %get-tuple-element.73), channel_id=1, source_target_pairs={{1,0},{2,1},{3,2},{4,3},{5,4},{6,5},{7,6},{8,7},{9,8},{10,9},{11,1... | collective-permute-start | bytes 983048 | tf_op jit(solution)/shard_map/ppermute | solution.py:18
  219.8 7.2 %collective-permute-start.20 = (f32[6,256]{1,0:T(8,128)S(1)}, f32[6,256]{1,0:T(8,128)S(1)}, u32[]{:S(2)}, u32[]{:S(2)}) collective-permute-start(f32[6,256]{1,0:T(8,128)S(1)} %fusion.28), channel_id=1, source_target_pairs={{0,2},{1,3},{2,0},{3,1},{4,6},{5,7},{6,4},{7,5},{8,10},{9,11},{10,... | collective-permute-start | bytes 18440 | tf_op jit(solution)/shard_map/ppermute | solution.py:67
  227.0 3.7 %collective-permute-start.21 = (f32[6,256]{1,0:T(8,128)S(1)}, f32[6,256]{1,0:T(8,128)S(1)}, u32[]{:S(2)}, u32[]{:S(2)}) collective-permute-start(f32[6,256]{1,0:T(8,128)S(1)} %add.67), channel_id=1, source_target_pairs={{0,4},{1,5},{2,6},{3,7},{4,0},{5,1},{6,2},{7,3},{8,12},{9,13},{10,... | collective-permute-start | bytes 18440 | tf_op jit(solution)/shard_map/ppermute | solution.py:67
  230.7 4.5 %collective-permute-start.22 = (f32[6,256]{1,0:T(8,128)S(1)}, f32[6,256]{1,0:T(8,128)S(1)}, u32[]{:S(2)}, u32[]{:S(2)}) collective-permute-start(f32[6,256]{1,0:T(8,128)S(1)} %add.68), channel_id=1, source_target_pairs={{0,8},{1,9},{2,10},{3,11},{4,12},{5,13},{6,14},{7,15},{8,0},{9,1},... | collective-permute-start | bytes 18440 | tf_op jit(solution)/shard_map/ppermute | solution.py:67
  (72 other events, 1611.1 us)
Sparse Core Ops, SparseCore 0:
  215.6 88.8 reduce-scatter.1
